TPU v7x, 128 devices: a whole 4x4x4 slice. The times are simulated.
128 devices in a mesh: tm: 4 (over x), space: 16 (over z, y), ens: 2 (over core).
Axes of the slice: x: 4, y: 4, z: 4, core: 2. Of those that a mesh axis runs over, the one named last changes fastest.
Arguments:
- start_states: float32 [4, 16, 1024, 1024], P('tm', 'ens', 'space'), may hold values from -6 to 6
- velocity_x: float32 [1024, 1024], P('space'), may hold values from -0.15 to 0.15
- velocity_y: float32 [1024, 1024], P('space'), may hold values from -0.15 to 0.15
- diffusivity: float32 [1024, 1024], P('space'), may hold values from 0.06 to 0.2
- source_shape: float32 [1024, 1024], P('space'), may hold values from -6 to 6
- params: float32 [16, 128], P('ens'), may hold values from -6 to 6
- obs_cell: int32 [4, 1024], P('tm', 'space'), may hold values from 0 to 1048575, as said below
- obs_data: float32 [4, 1024], P('tm', 'space'), may hold values from -6 to 6
- obs_noise: float32 [4, 1024, 16], P('tm', 'space'), may hold values from -6 to 6
- obs_var: float32 [4, 1024], P('tm', 'space'), may hold values from 0.05 to 0.5
Outputs:
- new_states: float32 [4, 16, 1024, 1024], P('tm', 'ens', 'space')
- new_params: float32 [16, 128], P('ens')
Inputs may be any that keep to these rules, and one draw needn't show every extreme that they name: `obs_cell`: entry (n, o) lies in the rows of slab o // 64, that is row (o // 64) * 64 up to 63 rows further.
All inputs are finite; a program needn't handle non-finite values.
Results may differ from a plain program's by a relative error of at most 0.0003.
Values sent between devices are 32-bit elements; how exact they have to be, the bound alone decides.
No kernel may reach another device: no remote copies, remote signals or barrier semaphores. Data moves between devices by JAX's collectives and lax.ppermute only.
A program may use at most 128 MiB of HBM per device.

v0:
```python
import math
import jax
import jax.numpy as jnp
from jax import lax
from jax.sharding import PartitionSpec as P

FINE = 4
FINE_DT = 0.25


def with_halo(cells, sides, width):
    for axis, dim in sides:
        count = lax.axis_size(axis)
        ends = count - 1
        head = lax.slice_in_dim(cells, 0, width, axis=dim)
        tail = lax.slice_in_dim(cells, cells.shape[dim] - width, cells.shape[dim], axis=dim)
        cells = jnp.concatenate(
            [
                lax.ppermute(tail, axis, [(i, (i + 1) % count) for i in range(ends)]),
                cells,
                lax.ppermute(head, axis, [((i + 1) % count, i) for i in range(ends)]),
            ],
            axis=dim,
        )
    return cells


def shifted(value, axis, steps):
    count = lax.axis_size(axis)
    first, last = (max(0, -steps), min(count, count - steps))
    return lax.ppermute(value, axis, [(source, source + steps) for source in range(first, last)])


def advance(values_in, coeffs, inside, step_size, forcing):
    middle = values_in[:, 1:-1, :]
    above_row = values_in[:, :-2, :]
    below_row = values_in[:, 2:, :]
    west_cell = jnp.pad(middle[:, :, :-1], ((0, 0), (0, 0), (1, 0)))
    east_cell = jnp.pad(middle[:, :, 1:], ((0, 0), (0, 0), (0, 1)))
    spread_term = coeffs[0] * (above_row + below_row + west_cell + east_cell - 4.0 * middle)
    tendency = (
        spread_term
        - coeffs[1] * (east_cell - west_cell) * 0.5
        - coeffs[2] * (below_row - above_row) * 0.5
    )
    if forcing is not None:
        tendency = tendency + forcing
    return (middle + step_size * tendency) * inside


def row_inside(first_row, count, total_rows):
    global_rows = first_row + jnp.arange(count, dtype=jnp.int32)
    return ((global_rows >= 0) & (global_rows < total_rows)).astype(jnp.float32)[:, None]


def per_device(
    start_states,
    velocity_x,
    velocity_y,
    diffusivity,
    source_shape,
    params,
    obs_cell,
    obs_data,
    obs_noise,
    obs_var,
):
    coarse_dt = FINE_DT * FINE
    state = start_states[0]
    members_here, row_count, col_count = state.shape
    slabs = row_count * lax.axis_size("space")
    first_row = lax.axis_index("space") * row_count
    slice_index = lax.axis_index("tm")
    band_width = col_count // params.shape[1]
    spread_params = jnp.repeat(params, band_width, axis=1)
    coeffs = jnp.stack([diffusivity, velocity_x, velocity_y])
    own_rows = row_inside(first_row, row_count, slabs)
    forcing = source_shape[None] * spread_params[:, None, :]
    current = state
    coarse_part = state
    for section in range(FINE):
        padded = with_halo(current, (("space", 1),), 1)
        if section == 0:
            coarse_part = advance(padded, coeffs, own_rows, coarse_dt, None)
        current = advance(padded, coeffs, own_rows, FINE_DT, forcing)
    correction = jnp.where(slice_index > 0, current - coarse_part, current)
    running = correction
    for link in range(lax.axis_size("tm") - 1):
        earlier = shifted(running, "tm", 1)
        padded = with_halo(earlier, (("space", 1),), 1)
        running = correction + advance(padded, coeffs, own_rows, coarse_dt, None)
    new_states = running[None]
    flat = running.reshape(members_here, row_count * col_count)
    local_cell = obs_cell[0] - first_row * col_count
    predicted = jnp.take(flat, local_cell, axis=1)
    every_pred, every_param = (
        lax.all_gather(predicted, "ens", axis=0, tiled=True),
        lax.all_gather(params, "ens", axis=0, tiled=True),
    )
    total = every_pred.shape[0]
    norm_factor = 1.0 / math.sqrt(total - 1)
    inv_spread = lax.rsqrt(obs_var[0])[None, :]
    pred_mean = jnp.mean(every_pred, axis=0, keepdims=True)
    anomaly = (every_pred - pred_mean) * (inv_spread * norm_factor)
    misfit = (obs_data[0][None, :] + obs_noise[0].T - every_pred) * inv_spread
    gram = jnp.dot(anomaly, anomaly.T, precision=lax.Precision.HIGHEST)
    cross = jnp.dot(anomaly, misfit.T, precision=lax.Precision.HIGHEST)
    gram, cross = lax.psum((gram, cross), ("tm", "space"))
    system = jnp.eye(total, dtype=jnp.float32) + gram
    factor = jnp.linalg.cholesky(system)
    weights = jax.scipy.linalg.cho_solve((factor, True), cross)
    param_anom = every_param - jnp.mean(every_param, axis=0)
    own_weights = lax.dynamic_slice_in_dim(
        weights, lax.axis_index("ens") * members_here, members_here, 1
    )
    new_params = (
        params + jnp.dot(own_weights.T, param_anom, precision=lax.Precision.HIGHEST) * norm_factor
    )
    return (new_states, new_params)


def solution(mesh):
    in_specs = (
        P("tm", "ens", "space", None),
        P("space", None),
        P("space", None),
        P("space", None),
        P("space", None),
        P("ens", None),
        P("tm", "space"),
        P("tm", "space"),
        P("tm", "space", None),
        P("tm", "space"),
    )
    out_specs = (P("tm", "ens", "space", None), P("ens", None))
    return jax.shard_map(
        per_device, mesh=mesh, in_specs=in_specs, out_specs=out_specs, check_vma=False
    )
```

profile of v0, /device:TPU:0, one launch (start us, length us, event | category | flops | bytes accessed | tf_op | source)
XLA Modules:
  0.0 608.6 jit_solution(10801937823309952952)
XLA Ops:
  1.7 3.6 collective-permute-start
  6.7 5.1 fusion.52
  14.2 3.4 fusion.2
  17.7 4.5 collective-permute-start.2
  24.4 3.7 collective-permute-done.3
  30.2 3.5 collective-permute-start.4
  35.8 4.6 collective-permute-done.5
  42.6 6.0 collective-permute-start.6
  51.0 3.7 collective-permute-done.7
  54.7 4.7 subtract_select_fusion
  59.4 3.5 collective-permute-start.8
  63.0 40.2 %collective-permute-done.8 = f32[8,64,1024]{2,1,0:T(8,128)S(1)} collective-permute-done((f32[8,64,1024]{2,1,0:T(8,128)S(1)}, f32[8,64,1024]{2,1,0:T(8,128)S(1)}, u32[]{:S(2)}, u32[]{:S(2)}) %collective-permute-start.8) | collective-permute-done | bytes 2097184 | tf_op jit(solution)/shard_map/ppermute | solution.py:31
  104.5 5.2 collective-permute-start.9
  113.2 4.7 collective-permute-start.11
  117.9 38.7 %collective-permute-done.11 = f32[8,64,1024]{2,1,0:T(8,128)S(1)} collective-permute-done((f32[8,64,1024]{2,1,0:T(8,128)S(1)}, f32[8,64,1024]{2,1,0:T(8,128)S(1)}, u32[]{:S(2)}, u32[]{:S(2)}) %collective-permute-start.11) | collective-permute-done | bytes 2097184 | tf_op jit(solution)/shard_map/ppermute | solution.py:31
  156.7 3.9 collective-permute-start.12
  162.8 3.7 collective-permute-done.13
  169.5 4.5 collective-permute-start.14
  175.9 34.7 %collective-permute-done.14 = f32[8,64,1024]{2,1,0:T(8,128)S(1)} collective-permute-done((f32[8,64,1024]{2,1,0:T(8,128)}, f32[8,64,1024]{2,1,0:T(8,128)S(1)}, u32[]{:S(2)}, u32[]{:S(2)}) %collective-permute-start.14) | collective-permute-done | bytes 2097184 | tf_op jit(solution)/shard_map/ppermute | solution.py:31
  210.6 5.4 collective-permute-start.15
  218.2 5.6 collective-permute-done.16
  226.7 17.9 %copy.18 = f32[8,64,1024]{0,2,1:T(8,128)} copy(f32[8,64,1024]{2,1,0:T(8,128)} %multiply_add_fusion.4) | data formatting | bytes 4194304 | tf_op jit(solution)/shard_map/add | solution.py:91
  244.6 11.1 %gather_fusion = f32[64,8]{1,0:T(8,128)S(1)} fusion(f32[8,65536]{0,1:T(8,128)} %bitcast.43, s32[1024]{0:T(1024)S(1)} %pad_clamp_fusion), kind=kCustom, calls=%fused_computation | custom fusion | bytes 4352 | tf_op jit(solution)/shard_map/jit(_take)/gather | solution.py:95
  258.0 345.3 %all-reduce.14 = (f32[16,16]{1,0:T(8,128)S(1)}, f32[16,16]{1,0:T(8,128)S(1)}) all-reduce(f32[16,16]{1,0:T(8,128)S(1)} %fusion.21, f32[16,16]{1,0:T(8,128)S(1)} %fusion.29), channel_id=1, replica_groups=mesh['tm'=4,'space'=16,'ens'=2] {'tm','space'}, use_global_device_ids=true, to_apply=%region_4.5 | all-reduce | flops 512 | bytes 4096 | tf_op jit(solution)/shard_map/psum | solution.py:108
  (90 shorter events, 40.2 us)
Async XLA Ops:
  1.7 12.4 %collective-permute-start = (f32[8,1,1024]{2,1,0:T(1,128)S(1)}, f32[8,1,1024]{2,1,0:T(1,128)S(1)}, u32[]{:S(2)}, u32[]{:S(2)}) collective-permute-start(f32[8,1,1024]{2,1,0:T(1,128)S(1)} %get-tuple-element.31), channel_id=1, source_target_pairs={{0,2},{2,4},{4,6},{6,8},{8,10},{10,12},{12,14},{14,16},{16,18},{18... | collective-permute-start | bytes 98312 | tf_op jit(solution)/shard_map/ppermute | solution.py:19
  5.3 8.9 %collective-permute-start.1 = (f32[8,1,1024]{2,1,0:T(1,128)S(1)}, f32[8,1,1024]{2,1,0:T(1,128)S(1)}, u32[]{:S(2)}, u32[]{:S(2)}) collective-permute-start(f32[8,1,1024]{2,1,0:T(1,128)S(1)} %get-tuple-element.30), channel_id=1, source_target_pairs={{2,0},{4,2},{6,4},{8,6},{10,8},{12,10},{14,12},{16,14},{18,16},{20... | collective-permute-start | bytes 98312 | tf_op jit(solution)/shard_map/ppermute | solution.py:21
  6.6 7.6 %copy-start = (f32[1,8,64,1024]{3,2,1,0:T(8,128)S(1)}, f32[1,8,64,1024]{3,2,1,0:T(8,128)}, u32[]{:S(2)}) copy-start(f32[1,8,64,1024]{3,2,1,0:T(8,128)} %param.10) | copy-start | bytes 6291460
  17.7 6.7 %collective-permute-start.2 = (f32[8,1,1024]{2,1,0:T(1,128)S(1)}, f32[8,1,1024]{2,1,0:T(1,128)S(1)}, u32[]{:S(2)}, u32[]{:S(2)}) collective-permute-start(f32[8,1,1024]{2,1,0:T(1,128)S(1)} %get-tuple-element.25), channel_id=1, source_target_pairs={{0,2},{2,4},{4,6},{6,8},{8,10},{10,12},{12,14},{14,16},{16,18},{18... | collective-permute-start | bytes 98312 | tf_op jit(solution)/shard_map/ppermute | solution.py:19
  22.3 5.8 collective-permute-start.3
  30.2 5.6 collective-permute-start.4
  33.7 6.8 %collective-permute-start.5 = (f32[8,1,1024]{2,1,0:T(1,128)S(1)}, f32[8,1,1024]{2,1,0:T(1,128)S(1)}, u32[]{:S(2)}, u32[]{:S(2)}) collective-permute-start(f32[8,1,1024]{2,1,0:T(1,128)S(1)} %get-tuple-element.20), channel_id=1, source_target_pairs={{2,0},{4,2},{6,4},{8,6},{10,8},{12,10},{14,12},{16,14},{18,16},{20... | collective-permute-start | bytes 98312 | tf_op jit(solution)/shard_map/ppermute | solution.py:21
  42.6 8.5 %collective-permute-start.6 = (f32[8,1,1024]{2,1,0:T(1,128)S(1)}, f32[8,1,1024]{2,1,0:T(1,128)S(1)}, u32[]{:S(2)}, u32[]{:S(2)}) collective-permute-start(f32[8,1,1024]{2,1,0:T(1,128)S(1)} %get-tuple-element.17), channel_id=1, source_target_pairs={{0,2},{2,4},{4,6},{6,8},{8,10},{10,12},{12,14},{14,16},{16,18},{18... | collective-permute-start | bytes 98312 | tf_op jit(solution)/shard_map/ppermute | solution.py:19
  48.6 6.1 collective-permute-start.7
  59.4 107.1 %copy-start.1 = (f32[8,64,1024]{2,1,0:T(8,128)}, f32[8,64,1024]{2,1,0:T(8,128)S(1)}, u32[]{:S(2)}) copy-start(f32[8,64,1024]{2,1,0:T(8,128)S(1)} %subtract_select_fusion) | copy-start | bytes 6291460
  59.4 43.7 %collective-permute-start.8 = (f32[8,64,1024]{2,1,0:T(8,128)S(1)}, f32[8,64,1024]{2,1,0:T(8,128)S(1)}, u32[]{:S(2)}, u32[]{:S(2)}) collective-permute-start(f32[8,64,1024]{2,1,0:T(8,128)S(1)} %subtract_select_fusion), channel_id=1, source_target_pairs={{0,32},{32,64},{64,96},{1,33},{33,65},{65,97},{2,34},{34,66},{66,9... | collective-permute-start | bytes 6291464 | tf_op jit(solution)/shard_map/ppermute | solution.py:31
  103.2 7.3 %collective-permute-start.10 = (f32[8,1,1024]{2,1,0:T(1,128)S(1)}, f32[8,1,1024]{2,1,0:T(1,128)S(1)}, u32[]{:S(2)}, u32[]{:S(2)}) collective-permute-start(f32[8,1,1024]{2,1,0:T(1,128)S(1)} %get-tuple-element.12), channel_id=1, source_target_pairs={{2,0},{4,2},{6,4},{8,6},{10,8},{12,10},{14,12},{16,14},{18,16},{20... | collective-permute-start | bytes 98312 | tf_op jit(solution)/shard_map/ppermute | solution.py:21
  104.5 6.8 %collective-permute-start.9 = (f32[8,1,1024]{2,1,0:T(1,128)S(1)}, f32[8,1,1024]{2,1,0:T(1,128)S(1)}, u32[]{:S(2)}, u32[]{:S(2)}) collective-permute-start(f32[8,1,1024]{2,1,0:T(1,128)S(1)} %get-tuple-element.13), channel_id=1, source_target_pairs={{0,2},{2,4},{4,6},{6,8},{8,10},{10,12},{12,14},{14,16},{16,18},{18... | collective-permute-start | bytes 98312 | tf_op jit(solution)/shard_map/ppermute | solution.py:19
  113.2 43.4 %collective-permute-start.11 = (f32[8,64,1024]{2,1,0:T(8,128)S(1)}, f32[8,64,1024]{2,1,0:T(8,128)S(1)}, u32[]{:S(2)}, u32[]{:S(2)}) collective-permute-start(f32[8,64,1024]{2,1,0:T(8,128)S(1)} %multiply_add_fusion.6), channel_id=1, source_target_pairs={{0,32},{32,64},{64,96},{1,33},{33,65},{65,97},{2,34},{34,66},{66,9... | collective-permute-start | bytes 6291464 | tf_op jit(solution)/shard_map/ppermute | solution.py:31
  156.7 6.1 collective-permute-start.12
  160.7 5.8 collective-permute-start.13
  166.5 9.3 %copy-start.12 = (s32[1,64]{1,0:T(1,128)S(1)}, s32[1,64]{1,0:T(1,128)}, u32[]{:S(2)}) copy-start(s32[1,64]{1,0:T(1,128)} %param.16) | copy-start | bytes 772
  166.5 9.4 %copy-start.13 = (f32[1,64]{1,0:T(1,128)S(1)}, f32[1,64]{1,0:T(1,128)}, u32[]{:S(2)}) copy-start(f32[1,64]{1,0:T(1,128)} %param.19) | copy-start | bytes 772
  169.5 41.1 %collective-permute-start.14 = (f32[8,64,1024]{2,1,0:T(8,128)}, f32[8,64,1024]{2,1,0:T(8,128)S(1)}, u32[]{:S(2)}, u32[]{:S(2)}) collective-permute-start(f32[8,64,1024]{2,1,0:T(8,128)} %multiply_add_fusion.5), channel_id=1, source_target_pairs={{0,32},{32,64},{64,96},{1,33},{33,65},{65,97},{2,34},{34,66},{66,9... | collective-permute-start | bytes 6291464 | tf_op jit(solution)/shard_map/ppermute | solution.py:31
  210.6 7.6 %collective-permute-start.15 = (f32[8,1,1024]{2,1,0:T(1,128)S(1)}, f32[8,1,1024]{2,1,0:T(1,128)S(1)}, u32[]{:S(2)}, u32[]{:S(2)}) collective-permute-start(f32[8,1,1024]{2,1,0:T(1,128)S(1)} %get-tuple-element.5), channel_id=1, source_target_pairs={{0,2},{2,4},{4,6},{6,8},{8,10},{10,12},{12,14},{14,16},{16,18},{18... | collective-permute-start | bytes 98312 | tf_op jit(solution)/shard_map/ppermute | solution.py:19
  216.0 7.8 %copy-start.2 = (f32[8,64,1024]{2,1,0:T(8,128)S(1)}, f32[8,64,1024]{2,1,0:T(8,128)}, u32[]{:S(2)}) copy-start(f32[8,64,1024]{2,1,0:T(8,128)} %copy-done.1) | copy-start | bytes 6291460
  216.1 7.8 %collective-permute-start.16 = (f32[8,1,1024]{2,1,0:T(1,128)S(1)}, f32[8,1,1024]{2,1,0:T(1,128)S(1)}, u32[]{:S(2)}, u32[]{:S(2)}) collective-permute-start(f32[8,1,1024]{2,1,0:T(1,128)S(1)} %get-tuple-element.4), channel_id=1, source_target_pairs={{2,0},{4,2},{6,4},{8,6},{10,8},{12,10},{14,12},{16,14},{18,16},{20... | collective-permute-start | bytes 98312 | tf_op jit(solution)/shard_map/ppermute | solution.py:21
  226.7 31.1 %copy-start.10 = (f32[1,64,16]{1,2,0:T(8,128)S(1)}, f32[1,64,16]{1,2,0:T(8,128)}, u32[]{:S(2)}) copy-start(f32[1,64,16]{1,2,0:T(8,128)} %param.18) | copy-start | bytes 12292
  226.7 31.1 %copy-start.11 = (f32[1,64]{1,0:T(1,128)S(1)}, f32[1,64]{1,0:T(1,128)}, u32[]{:S(2)}) copy-start(f32[1,64]{1,0:T(1,128)} %param.17) | copy-start | bytes 772
  (7 other events, 47.6 us)
where the time goes:
time: 610 us; the launch traced here: 609 us
  blocking collectives  349 us (57%)
  waiting for transfers between devices  135 us (22%)
  starting transfers between devices  54.3 us (9%)
  local copies, waits for them, and re-layouts  43 us (7%)
  other arithmetic  24.3 us (4%)
    psum x1, blocking collectives, per_device(): gram, cross = lax.psum((gram, cross), ('tm', 'space'))  345 us
    ppermute x3, waiting for transfers between devices, shifted(): lax.ppermute(value, axis, [(source, source + steps) for source in range(f...  114 us
    ppermute x7, starting transfers between devices, with_halo(): lax.ppermute(tail, axis, [(i, (i + 1) % count) for i in range(ends)])  32.1 us
    ppermute x7, waiting for transfers between devices, with_halo(): lax.ppermute(head, axis, [((i + 1) % count, i) for i in range(ends)])  21.2 us
    add x1, local copies, waits for them, and re-layouts, per_device(): running = correction + advance(padded, coeffs, own_rows, coarse_dt, None)  17.9 us
    ppermute x3, starting transfers between devices, shifted(): lax.ppermute(value, axis, [(source, source + steps) for source in range(f...  12.7 us
  transfers between devices with their start and end apart: 17, of which 9 were waited for; matrix products, arithmetic and copies ran while one was open for 2% of the time, Pallas kernels for 0%

commit v1 on v0

--- a/solution.py
+++ b/solution.py
@@ -105,7 +105,15 @@
     misfit = (obs_data[0][None, :] + obs_noise[0].T - every_pred) * inv_spread
     gram = jnp.dot(anomaly, anomaly.T, precision=lax.Precision.HIGHEST)
     cross = jnp.dot(anomaly, misfit.T, precision=lax.Precision.HIGHEST)
-    gram, cross = lax.psum((gram, cross), ("tm", "space"))
+
+    def save_cube(piece_in):
+        axis_name = "tm"
+        chip_axis = "space"
+        for src_i in (chip_axis, axis_name):
+            piece_in = lax.psum(piece_in, src_i)
+        return piece_in
+
+    gram, cross = save_cube((gram, cross))
     system = jnp.eye(total, dtype=jnp.float32) + gram
     factor = jnp.linalg.cholesky(system)
     weights = jax.scipy.linalg.cho_solve((factor, True), cross)

time: 610 us -> 355 us (0.58)
  blocking collectives: 349 us -> 94.6 us
    psum x1 -> x2, blocking collectives: 345 us -> 91 us  [save_cube(): piece_in = lax.psum(piece_in, src_i)]
  transfers between devices with their start and end apart: 17 -> 17, of which waited for: 9 -> 9; matrix products, arithmetic and copies ran while one was open for 2% -> 4% of each run, Pallas kernels for 0% -> 0%
where the time goes in v1:
time: 355 us; the launch traced here: 354 us
  waiting for transfers between devices  135 us (38%)
  blocking collectives  94.6 us (27%)
  starting transfers between devices  54.3 us (15%)
  local copies, waits for them, and re-layouts  43.1 us (12%)
  other arithmetic  24.3 us (7%)
    ppermute x3, waiting for transfers between devices, shifted(): lax.ppermute(value, axis, [(source, source + steps) for source in range(f...  114 us
    psum x2, blocking collectives, save_cube(): piece_in = lax.psum(piece_in, src_i)  91 us
    ppermute x7, starting transfers between devices, with_halo(): lax.ppermute(tail, axis, [(i, (i + 1) % count) for i in range(ends)])  32.1 us
    ppermute x7, waiting for transfers between devices, with_halo(): lax.ppermute(head, axis, [((i + 1) % count, i) for i in range(ends)])  21.2 us
    add x1, local copies, waits for them, and re-layouts, per_device(): running = correction + advance(padded, coeffs, own_rows, coarse_dt, None)  18 us
    ppermute x3, starting transfers between devices, shifted(): lax.ppermute(value, axis, [(source, source + steps) for source in range(f...  12.7 us
    gather x1, local copies, waits for them, and re-layouts, per_device(): predicted = jnp.take(flat, local_cell, axis=1)  11.1 us
    slice x7, local copies, waits for them, and re-layouts, advance(): west_cell = jnp.pad(middle[:, :, :-1], ((0, 0), (0, 0), (1, 0)))  10.1 us
  transfers between devices with their start and end apart: 17, of which 9 were waited for; matrix products, arithmetic and copies ran while one was open for 4% of the time, Pallas kernels for 0%

profile of v1, /device:TPU:0, one launch (start us, length us, event | category | flops | bytes accessed | tf_op | source)
XLA Modules:
  0.0 354.4 jit_solution(13164018722612879295)
XLA Ops:
  1.7 3.6 %collective-permute-start = (f32[8,1,1024]{2,1,0:T(1,128)S(1)}, f32[8,1,1024]{2,1,0:T(1,128)S(1)}, u32[]{:S(2)}, u32[]{:S(2)}) collective-permute-start(f32[8,1,1024]{2,1,0:T(1,128)S(1)} %get-tuple-element.33), channel_id=1, source_target_pairs={{0,2},{2,4},{4,6},{6,8},{8,10},{10,12},{12,14},{14,16},{16,18},{18... | collective-permute-start | bytes 98312 | tf_op jit(solution)/shard_map/ppermute | solution.py:19
  6.7 5.1 %fusion.52 = (f32[8,64,1023]{2,1,0:T(8,128)}, f32[8,64,1023]{2,1,0:T(8,128)}) fusion(f32[8,64,1024]{2,1,0:T(8,128)} %bitcast.40), kind=kLoop, calls=%fused_computation.96 | loop fusion | bytes 8380416 | tf_op jit(solution)/shard_map/slice | solution.py:38
  17.7 4.5 %collective-permute-start.2 = (f32[8,1,1024]{2,1,0:T(1,128)S(1)}, f32[8,1,1024]{2,1,0:T(1,128)S(1)}, u32[]{:S(2)}, u32[]{:S(2)}) collective-permute-start(f32[8,1,1024]{2,1,0:T(1,128)S(1)} %get-tuple-element.27), channel_id=1, source_target_pairs={{0,2},{2,4},{4,6},{6,8},{8,10},{10,12},{12,14},{14,16},{16,18},{18... | collective-permute-start | bytes 98312 | tf_op jit(solution)/shard_map/ppermute | solution.py:19
  24.4 3.7 %collective-permute-done.3 = f32[8,1,1024]{2,1,0:T(1,128)S(1)} collective-permute-done((f32[8,1,1024]{2,1,0:T(1,128)S(1)}, f32[8,1,1024]{2,1,0:T(1,128)S(1)}, u32[]{:S(2)}, u32[]{:S(2)}) %collective-permute-start.3) | collective-permute-done | bytes 32800 | tf_op jit(solution)/shard_map/ppermute | solution.py:21
  30.2 3.5 collective-permute-start.4
  35.8 4.6 %collective-permute-done.5 = f32[8,1,1024]{2,1,0:T(1,128)S(1)} collective-permute-done((f32[8,1,1024]{2,1,0:T(1,128)S(1)}, f32[8,1,1024]{2,1,0:T(1,128)S(1)}, u32[]{:S(2)}, u32[]{:S(2)}) %collective-permute-start.5) | collective-permute-done | bytes 32800 | tf_op jit(solution)/shard_map/ppermute | solution.py:21
  42.6 6.0 %collective-permute-start.6 = (f32[8,1,1024]{2,1,0:T(1,128)S(1)}, f32[8,1,1024]{2,1,0:T(1,128)S(1)}, u32[]{:S(2)}, u32[]{:S(2)}) collective-permute-start(f32[8,1,1024]{2,1,0:T(1,128)S(1)} %get-tuple-element.19), channel_id=1, source_target_pairs={{0,2},{2,4},{4,6},{6,8},{8,10},{10,12},{12,14},{14,16},{16,18},{18... | collective-permute-start | bytes 98312 | tf_op jit(solution)/shard_map/ppermute | solution.py:19
  51.0 3.7 %collective-permute-done.7 = f32[8,1,1024]{2,1,0:T(1,128)S(1)} collective-permute-done((f32[8,1,1024]{2,1,0:T(1,128)S(1)}, f32[8,1,1024]{2,1,0:T(1,128)S(1)}, u32[]{:S(2)}, u32[]{:S(2)}) %collective-permute-start.7) | collective-permute-done | bytes 32800 | tf_op jit(solution)/shard_map/ppermute | solution.py:21
  54.7 4.7 %subtract_select_fusion = f32[8,64,1024]{2,1,0:T(8,128)S(1)} fusion(f32[8,64,1024]{2,1,0:T(8,128)S(1)} %fusion.8, f32[8,64,1024]{2,1,0:T(8,128)S(1)} %bitcast.42, f32[8,64,1023]{2,1,0:T(8,128)S(1)} %get-tuple-element.21, f32[8,64,1023]{2,1,0:T(8,128)S(1)} %get-tuple-element.20, f32[8,1,1024]{2,1,0:T(1,128)S(1)} %collective-permute-done.6, ...), kind=kLoop, calls=%fused_computation.5 | loop fusion | flops 21495808 | bytes 15884545 | tf_op jit(solution)/shard_map/jit(_where)/select_n | solution.py:86
  59.4 3.5 collective-permute-start.8
  63.0 40.2 %collective-permute-done.8 = f32[8,64,1024]{2,1,0:T(8,128)S(1)} collective-permute-done((f32[8,64,1024]{2,1,0:T(8,128)S(1)}, f32[8,64,1024]{2,1,0:T(8,128)S(1)}, u32[]{:S(2)}, u32[]{:S(2)}) %collective-permute-start.8) | collective-permute-done | bytes 2097184 | tf_op jit(solution)/shard_map/ppermute | solution.py:31
  104.5 5.2 %collective-permute-start.9 = (f32[8,1,1024]{2,1,0:T(1,128)S(1)}, f32[8,1,1024]{2,1,0:T(1,128)S(1)}, u32[]{:S(2)}, u32[]{:S(2)}) collective-permute-start(f32[8,1,1024]{2,1,0:T(1,128)S(1)} %get-tuple-element.15), channel_id=1, source_target_pairs={{0,2},{2,4},{4,6},{6,8},{8,10},{10,12},{12,14},{14,16},{16,18},{18... | collective-permute-start | bytes 98312 | tf_op jit(solution)/shard_map/ppermute | solution.py:19
  113.2 4.7 %collective-permute-start.11 = (f32[8,64,1024]{2,1,0:T(8,128)S(1)}, f32[8,64,1024]{2,1,0:T(8,128)S(1)}, u32[]{:S(2)}, u32[]{:S(2)}) collective-permute-start(f32[8,64,1024]{2,1,0:T(8,128)S(1)} %multiply_add_fusion.6), channel_id=1, source_target_pairs={{0,32},{32,64},{64,96},{1,33},{33,65},{65,97},{2,34},{34,66},{66,9... | collective-permute-start | bytes 6291464 | tf_op jit(solution)/shard_map/ppermute | solution.py:31
  118.0 38.7 %collective-permute-done.11 = f32[8,64,1024]{2,1,0:T(8,128)S(1)} collective-permute-done((f32[8,64,1024]{2,1,0:T(8,128)S(1)}, f32[8,64,1024]{2,1,0:T(8,128)S(1)}, u32[]{:S(2)}, u32[]{:S(2)}) %collective-permute-start.11) | collective-permute-done | bytes 2097184 | tf_op jit(solution)/shard_map/ppermute | solution.py:31
  156.7 3.9 %collective-permute-start.12 = (f32[8,1,1024]{2,1,0:T(1,128)S(1)}, f32[8,1,1024]{2,1,0:T(1,128)S(1)}, u32[]{:S(2)}, u32[]{:S(2)}) collective-permute-start(f32[8,1,1024]{2,1,0:T(1,128)S(1)} %get-tuple-element.11), channel_id=1, source_target_pairs={{0,2},{2,4},{4,6},{6,8},{8,10},{10,12},{12,14},{14,16},{16,18},{18... | collective-permute-start | bytes 98312 | tf_op jit(solution)/shard_map/ppermute | solution.py:19
  162.8 3.7 %collective-permute-done.13 = f32[8,1,1024]{2,1,0:T(1,128)S(1)} collective-permute-done((f32[8,1,1024]{2,1,0:T(1,128)S(1)}, f32[8,1,1024]{2,1,0:T(1,128)S(1)}, u32[]{:S(2)}, u32[]{:S(2)}) %collective-permute-start.13) | collective-permute-done | bytes 32800 | tf_op jit(solution)/shard_map/ppermute | solution.py:21
  169.5 4.5 %collective-permute-start.14 = (f32[8,64,1024]{2,1,0:T(8,128)}, f32[8,64,1024]{2,1,0:T(8,128)S(1)}, u32[]{:S(2)}, u32[]{:S(2)}) collective-permute-start(f32[8,64,1024]{2,1,0:T(8,128)} %multiply_add_fusion.5), channel_id=1, source_target_pairs={{0,32},{32,64},{64,96},{1,33},{33,65},{65,97},{2,34},{34,66},{66,9... | collective-permute-start | bytes 6291464 | tf_op jit(solution)/shard_map/ppermute | solution.py:31
  175.9 34.7 %collective-permute-done.14 = f32[8,64,1024]{2,1,0:T(8,128)S(1)} collective-permute-done((f32[8,64,1024]{2,1,0:T(8,128)}, f32[8,64,1024]{2,1,0:T(8,128)S(1)}, u32[]{:S(2)}, u32[]{:S(2)}) %collective-permute-start.14) | collective-permute-done | bytes 2097184 | tf_op jit(solution)/shard_map/ppermute | solution.py:31
  210.6 5.4 %collective-permute-start.15 = (f32[8,1,1024]{2,1,0:T(1,128)S(1)}, f32[8,1,1024]{2,1,0:T(1,128)S(1)}, u32[]{:S(2)}, u32[]{:S(2)}) collective-permute-start(f32[8,1,1024]{2,1,0:T(1,128)S(1)} %get-tuple-element.7), channel_id=1, source_target_pairs={{0,2},{2,4},{4,6},{6,8},{8,10},{10,12},{12,14},{14,16},{16,18},{18... | collective-permute-start | bytes 98312 | tf_op jit(solution)/shard_map/ppermute | solution.py:19
  218.2 5.6 %collective-permute-done.16 = f32[8,1,1024]{2,1,0:T(1,128)S(1)} collective-permute-done((f32[8,1,1024]{2,1,0:T(1,128)S(1)}, f32[8,1,1024]{2,1,0:T(1,128)S(1)}, u32[]{:S(2)}, u32[]{:S(2)}) %collective-permute-start.16) | collective-permute-done | bytes 32800 | tf_op jit(solution)/shard_map/ppermute | solution.py:21
  226.7 18.0 %copy.18 = f32[8,64,1024]{0,2,1:T(8,128)} copy(f32[8,64,1024]{2,1,0:T(8,128)} %multiply_add_fusion.4) | data formatting | bytes 4194304 | tf_op jit(solution)/shard_map/add | solution.py:91
  244.7 11.1 %gather_fusion = f32[64,8]{1,0:T(8,128)S(1)} fusion(f32[8,65536]{0,1:T(8,128)} %bitcast.43, s32[1024]{0:T(1024)S(1)} %pad_clamp_fusion), kind=kCustom, calls=%fused_computation | custom fusion | bytes 4352 | tf_op jit(solution)/shard_map/jit(_take)/gather | solution.py:95
  258.1 73.2 %all-reduce.14 = (f32[16,16]{1,0:T(8,128)S(1)}, f32[16,16]{1,0:T(8,128)S(1)}) all-reduce(f32[16,16]{1,0:T(8,128)S(1)} %fusion.21, f32[16,16]{1,0:T(8,128)S(1)} %fusion.29), channel_id=1, replica_groups=mesh['tm'=4,'space'=16,'ens'=2] {'space'}, use_global_device_ids=true, to_apply=%region_5.6 | all-reduce | flops 512 | bytes 4096 | tf_op jit(solution)/shard_map/psum | solution.py:113
  331.3 17.8 %all-reduce.15 = (f32[16,16]{1,0:T(8,128)S(1)}, f32[16,16]{1,0:T(8,128)S(1)}) all-reduce(f32[16,16]{1,0:T(8,128)S(1)} %get-tuple-element.2, f32[16,16]{1,0:T(8,128)S(1)} %get-tuple-element.3), channel_id=1, replica_groups=mesh['tm'=4,'space'=16,'ens'=2] {'tm'}, use_global_device_ids=true, to_apply=%region_6.7 | all-reduce | flops 512 | bytes 4096 | tf_op jit(solution)/shard_map/psum | solution.py:113
  (91 shorter events, 43.6 us)
Async XLA Ops:
  1.7 12.4 %collective-permute-start = (f32[8,1,1024]{2,1,0:T(1,128)S(1)}, f32[8,1,1024]{2,1,0:T(1,128)S(1)}, u32[]{:S(2)}, u32[]{:S(2)}) collective-permute-start(f32[8,1,1024]{2,1,0:T(1,128)S(1)} %get-tuple-element.33), channel_id=1, source_target_pairs={{0,2},{2,4},{4,6},{6,8},{8,10},{10,12},{12,14},{14,16},{16,18},{18... | collective-permute-start | bytes 98312 | tf_op jit(solution)/shard_map/ppermute | solution.py:19
  5.3 8.9 %collective-permute-start.1 = (f32[8,1,1024]{2,1,0:T(1,128)S(1)}, f32[8,1,1024]{2,1,0:T(1,128)S(1)}, u32[]{:S(2)}, u32[]{:S(2)}) collective-permute-start(f32[8,1,1024]{2,1,0:T(1,128)S(1)} %get-tuple-element.32), channel_id=1, source_target_pairs={{2,0},{4,2},{6,4},{8,6},{10,8},{12,10},{14,12},{16,14},{18,16},{20... | collective-permute-start | bytes 98312 | tf_op jit(solution)/shard_map/ppermute | solution.py:21
  6.6 7.6 %copy-start = (f32[1,8,64,1024]{3,2,1,0:T(8,128)S(1)}, f32[1,8,64,1024]{3,2,1,0:T(8,128)}, u32[]{:S(2)}) copy-start(f32[1,8,64,1024]{3,2,1,0:T(8,128)} %param.10) | copy-start | bytes 6291460
  17.7 6.7 %collective-permute-start.2 = (f32[8,1,1024]{2,1,0:T(1,128)S(1)}, f32[8,1,1024]{2,1,0:T(1,128)S(1)}, u32[]{:S(2)}, u32[]{:S(2)}) collective-permute-start(f32[8,1,1024]{2,1,0:T(1,128)S(1)} %get-tuple-element.27), channel_id=1, source_target_pairs={{0,2},{2,4},{4,6},{6,8},{8,10},{10,12},{12,14},{14,16},{16,18},{18... | collective-permute-start | bytes 98312 | tf_op jit(solution)/shard_map/ppermute | solution.py:19
  22.3 5.8 %collective-permute-start.3 = (f32[8,1,1024]{2,1,0:T(1,128)S(1)}, f32[8,1,1024]{2,1,0:T(1,128)S(1)}, u32[]{:S(2)}, u32[]{:S(2)}) collective-permute-start(f32[8,1,1024]{2,1,0:T(1,128)S(1)} %get-tuple-element.26), channel_id=1, source_target_pairs={{2,0},{4,2},{6,4},{8,6},{10,8},{12,10},{14,12},{16,14},{18,16},{20... | collective-permute-start | bytes 98312 | tf_op jit(solution)/shard_map/ppermute | solution.py:21
  30.2 5.6 %collective-permute-start.4 = (f32[8,1,1024]{2,1,0:T(1,128)S(1)}, f32[8,1,1024]{2,1,0:T(1,128)S(1)}, u32[]{:S(2)}, u32[]{:S(2)}) collective-permute-start(f32[8,1,1024]{2,1,0:T(1,128)S(1)} %get-tuple-element.23), channel_id=1, source_target_pairs={{0,2},{2,4},{4,6},{6,8},{8,10},{10,12},{12,14},{14,16},{16,18},{18... | collective-permute-start | bytes 98312 | tf_op jit(solution)/shard_map/ppermute | solution.py:19
  33.7 6.8 %collective-permute-start.5 = (f32[8,1,1024]{2,1,0:T(1,128)S(1)}, f32[8,1,1024]{2,1,0:T(1,128)S(1)}, u32[]{:S(2)}, u32[]{:S(2)}) collective-permute-start(f32[8,1,1024]{2,1,0:T(1,128)S(1)} %get-tuple-element.22), channel_id=1, source_target_pairs={{2,0},{4,2},{6,4},{8,6},{10,8},{12,10},{14,12},{16,14},{18,16},{20... | collective-permute-start | bytes 98312 | tf_op jit(solution)/shard_map/ppermute | solution.py:21
  42.6 8.5 %collective-permute-start.6 = (f32[8,1,1024]{2,1,0:T(1,128)S(1)}, f32[8,1,1024]{2,1,0:T(1,128)S(1)}, u32[]{:S(2)}, u32[]{:S(2)}) collective-permute-start(f32[8,1,1024]{2,1,0:T(1,128)S(1)} %get-tuple-element.19), channel_id=1, source_target_pairs={{0,2},{2,4},{4,6},{6,8},{8,10},{10,12},{12,14},{14,16},{16,18},{18... | collective-permute-start | bytes 98312 | tf_op jit(solution)/shard_map/ppermute | solution.py:19
  48.6 6.1 %collective-permute-start.7 = (f32[8,1,1024]{2,1,0:T(1,128)S(1)}, f32[8,1,1024]{2,1,0:T(1,128)S(1)}, u32[]{:S(2)}, u32[]{:S(2)}) collective-permute-start(f32[8,1,1024]{2,1,0:T(1,128)S(1)} %get-tuple-element.18), channel_id=1, source_target_pairs={{2,0},{4,2},{6,4},{8,6},{10,8},{12,10},{14,12},{16,14},{18,16},{20... | collective-permute-start | bytes 98312 | tf_op jit(solution)/shard_map/ppermute | solution.py:21
  59.4 107.1 %copy-start.1 = (f32[8,64,1024]{2,1,0:T(8,128)}, f32[8,64,1024]{2,1,0:T(8,128)S(1)}, u32[]{:S(2)}) copy-start(f32[8,64,1024]{2,1,0:T(8,128)S(1)} %subtract_select_fusion) | copy-start | bytes 6291460
  59.4 43.7 %collective-permute-start.8 = (f32[8,64,1024]{2,1,0:T(8,128)S(1)}, f32[8,64,1024]{2,1,0:T(8,128)S(1)}, u32[]{:S(2)}, u32[]{:S(2)}) collective-permute-start(f32[8,64,1024]{2,1,0:T(8,128)S(1)} %subtract_select_fusion), channel_id=1, source_target_pairs={{0,32},{32,64},{64,96},{1,33},{33,65},{65,97},{2,34},{34,66},{66,9... | collective-permute-start | bytes 6291464 | tf_op jit(solution)/shard_map/ppermute | solution.py:31
  103.2 7.3 %collective-permute-start.10 = (f32[8,1,1024]{2,1,0:T(1,128)S(1)}, f32[8,1,1024]{2,1,0:T(1,128)S(1)}, u32[]{:S(2)}, u32[]{:S(2)}) collective-permute-start(f32[8,1,1024]{2,1,0:T(1,128)S(1)} %get-tuple-element.14), channel_id=1, source_target_pairs={{2,0},{4,2},{6,4},{8,6},{10,8},{12,10},{14,12},{16,14},{18,16},{20... | collective-permute-start | bytes 98312 | tf_op jit(solution)/shard_map/ppermute | solution.py:21
  104.5 6.8 %collective-permute-start.9 = (f32[8,1,1024]{2,1,0:T(1,128)S(1)}, f32[8,1,1024]{2,1,0:T(1,128)S(1)}, u32[]{:S(2)}, u32[]{:S(2)}) collective-permute-start(f32[8,1,1024]{2,1,0:T(1,128)S(1)} %get-tuple-element.15), channel_id=1, source_target_pairs={{0,2},{2,4},{4,6},{6,8},{8,10},{10,12},{12,14},{14,16},{16,18},{18... | collective-permute-start | bytes 98312 | tf_op jit(solution)/shard_map/ppermute | solution.py:19
  113.2 43.4 %collective-permute-start.11 = (f32[8,64,1024]{2,1,0:T(8,128)S(1)}, f32[8,64,1024]{2,1,0:T(8,128)S(1)}, u32[]{:S(2)}, u32[]{:S(2)}) collective-permute-start(f32[8,64,1024]{2,1,0:T(8,128)S(1)} %multiply_add_fusion.6), channel_id=1, source_target_pairs={{0,32},{32,64},{64,96},{1,33},{33,65},{65,97},{2,34},{34,66},{66,9... | collective-permute-start | bytes 6291464 | tf_op jit(solution)/shard_map/ppermute | solution.py:31
  156.7 6.1 %collective-permute-start.12 = (f32[8,1,1024]{2,1,0:T(1,128)S(1)}, f32[8,1,1024]{2,1,0:T(1,128)S(1)}, u32[]{:S(2)}, u32[]{:S(2)}) collective-permute-start(f32[8,1,1024]{2,1,0:T(1,128)S(1)} %get-tuple-element.11), channel_id=1, source_target_pairs={{0,2},{2,4},{4,6},{6,8},{8,10},{10,12},{12,14},{14,16},{16,18},{18... | collective-permute-start | bytes 98312 | tf_op jit(solution)/shard_map/ppermute | solution.py:19
  160.7 5.8 %collective-permute-start.13 = (f32[8,1,1024]{2,1,0:T(1,128)S(1)}, f32[8,1,1024]{2,1,0:T(1,128)S(1)}, u32[]{:S(2)}, u32[]{:S(2)}) collective-permute-start(f32[8,1,1024]{2,1,0:T(1,128)S(1)} %get-tuple-element.10), channel_id=1, source_target_pairs={{2,0},{4,2},{6,4},{8,6},{10,8},{12,10},{14,12},{16,14},{18,16},{20... | collective-permute-start | bytes 98312 | tf_op jit(solution)/shard_map/ppermute | solution.py:21
  166.5 9.3 %copy-start.12 = (s32[1,64]{1,0:T(1,128)S(1)}, s32[1,64]{1,0:T(1,128)}, u32[]{:S(2)}) copy-start(s32[1,64]{1,0:T(1,128)} %param.16) | copy-start | bytes 772
  166.5 9.4 %copy-start.13 = (f32[1,64]{1,0:T(1,128)S(1)}, f32[1,64]{1,0:T(1,128)}, u32[]{:S(2)}) copy-start(f32[1,64]{1,0:T(1,128)} %param.19) | copy-start | bytes 772
  169.5 41.1 %collective-permute-start.14 = (f32[8,64,1024]{2,1,0:T(8,128)}, f32[8,64,1024]{2,1,0:T(8,128)S(1)}, u32[]{:S(2)}, u32[]{:S(2)}) collective-permute-start(f32[8,64,1024]{2,1,0:T(8,128)} %multiply_add_fusion.5), channel_id=1, source_target_pairs={{0,32},{32,64},{64,96},{1,33},{33,65},{65,97},{2,34},{34,66},{66,9... | collective-permute-start | bytes 6291464 | tf_op jit(solution)/shard_map/ppermute | solution.py:31
  210.6 7.6 %collective-permute-start.15 = (f32[8,1,1024]{2,1,0:T(1,128)S(1)}, f32[8,1,1024]{2,1,0:T(1,128)S(1)}, u32[]{:S(2)}, u32[]{:S(2)}) collective-permute-start(f32[8,1,1024]{2,1,0:T(1,128)S(1)} %get-tuple-element.7), channel_id=1, source_target_pairs={{0,2},{2,4},{4,6},{6,8},{8,10},{10,12},{12,14},{14,16},{16,18},{18... | collective-permute-start | bytes 98312 | tf_op jit(solution)/shard_map/ppermute | solution.py:19
  216.0 7.8 %copy-start.2 = (f32[8,64,1024]{2,1,0:T(8,128)S(1)}, f32[8,64,1024]{2,1,0:T(8,128)}, u32[]{:S(2)}) copy-start(f32[8,64,1024]{2,1,0:T(8,128)} %copy-done.1) | copy-start | bytes 6291460
  216.1 7.8 %collective-permute-start.16 = (f32[8,1,1024]{2,1,0:T(1,128)S(1)}, f32[8,1,1024]{2,1,0:T(1,128)S(1)}, u32[]{:S(2)}, u32[]{:S(2)}) collective-permute-start(f32[8,1,1024]{2,1,0:T(1,128)S(1)} %get-tuple-element.6), channel_id=1, source_target_pairs={{2,0},{4,2},{6,4},{8,6},{10,8},{12,10},{14,12},{16,14},{18,16},{20... | collective-permute-start | bytes 98312 | tf_op jit(solution)/shard_map/ppermute | solution.py:21
  226.7 31.2 %copy-start.10 = (f32[1,64,16]{1,2,0:T(8,128)S(1)}, f32[1,64,16]{1,2,0:T(8,128)}, u32[]{:S(2)}) copy-start(f32[1,64,16]{1,2,0:T(8,128)} %param.18) | copy-start | bytes 12292
  226.7 31.2 %copy-start.11 = (f32[1,64]{1,0:T(1,128)S(1)}, f32[1,64]{1,0:T(1,128)}, u32[]{:S(2)}) copy-start(f32[1,64]{1,0:T(1,128)} %param.17) | copy-start | bytes 772
  (7 other events, 47.6 us)
